TPU v7x, 256 devices: a whole 4x4x8 slice. The times are simulated.
256 devices in a mesh: dp: 32 (over x, y, core), shard: 8 (over z).
Axes of the slice: x: 4, y: 4, z: 8, core: 2. Of those that a mesh axis runs over, the one named last changes fastest.
Arguments:
- audio: bfloat16 [65536, 512], P(('dp', 'shard')), may hold values from -6 to 6
- cotangent: bfloat16 [65536, 512], P(('dp', 'shard')), may hold values from -6 to 6
- clip_lengths: int32 [256, 8], P(('dp', 'shard')), may hold values from 1 to 128, 256 in all within a row
- conv_weight: bfloat16 [3584, 512], P('shard'), may hold values from -0.09375 to 0.09375
- mix_weight: bfloat16 [512, 512], P('shard'), may hold values from -0.25 to 0.25
- conv_bias: float32 [512], replicated, may hold values from -3 to 3
- alpha_in: float32 [512], replicated, may hold values from 0.5 to 3
- alpha_mid: float32 [512], replicated, may hold values from 0.5 to 3
Outputs:
- in_grad: bfloat16 [65536, 512], P(('dp', 'shard'))
- conv_grad: float32 [3584, 512], P(('dp', 'shard'))
- mix_grad: float32 [512, 512], P(('dp', 'shard'))
- vector_grad: float32 [4, 512], P(None, ('dp', 'shard'))
Inputs may be any that keep to these rules, and one draw needn't show every extreme that they name: `clip_lengths`: each device's clip lengths sum to 256; the largest on each device is 128.
All inputs are finite; a program needn't handle non-finite values.
Results may differ from a plain program's by a relative error of at most 0.01.
Values may be sent and summed in bfloat16 or wider, within the bound.
No kernel may reach another device: no remote copies, remote signals or barrier semaphores. Data moves between devices by JAX's collectives and lax.ppermute only.
A program may use at most 64 MiB of HBM per device.

v0:
```python
import jax
import jax.numpy as jnp
from jax import lax
from jax.sharding import Mesh, PartitionSpec as P

C = 512
TAPS = 7
DILATION_SIZE = 9
FRAME_AXES = ("x", "y", "c", "z")
SCATTER_ORDER = ("c", "z", "y", "x")
EXTRA_COLUMNS = 128


def shift_rows(block, tap_offset, fill):
    rows = block.shape[0]
    shift_amount = min(abs(tap_offset), rows)
    if shift_amount == 0:
        return block
    edge_padding = jnp.full((shift_amount,) + block.shape[1:], fill, block.dtype)
    if tap_offset > 0:
        return jnp.concatenate([block[shift_amount:], edge_padding], axis=0)
    return jnp.concatenate([edge_padding, block[: rows - shift_amount]], axis=0)


def clip_masks(lengths_row, rows):
    clip_ends = jnp.cumsum(lengths_row)
    position = jnp.arange(rows, dtype=jnp.int32)
    clip_id = jnp.sum((position[:, None] >= clip_ends[None, :]).astype(jnp.int32), axis=1)
    result = []
    for kernel_tap_index in range(TAPS):
        tap_offset = (kernel_tap_index - 3) * DILATION_SIZE
        result.append(shift_rows(clip_id, tap_offset, -1) == clip_id)
    return result


def snake_parts(value, alpha):
    sine = jnp.sin(alpha * value)
    double = jnp.sin(2.0 * alpha * value)
    return (
        value + sine * sine / alpha,
        1.0 + double,
        value * double / alpha - sine * sine / (alpha * alpha),
    )


def permute_scatter(value, axis):
    n = lax.axis_size(axis)
    me = lax.axis_index(axis)
    each = value.shape[0] // n
    total = lax.dynamic_slice_in_dim(value, me * each, each)
    for step in range(1, n):
        chunk = lax.dynamic_slice_in_dim(value, (me + step) % n * each, each)
        total = total + lax.ppermute(chunk, axis, [(j, (j + step) % n) for j in range(n)])
    return total


def per_device(
    audio, cotangent, clip_lengths, conv_weight, mix_weight, conv_bias, alpha_in, alpha_mid
):
    rows = audio.shape[0]
    same_clip_flags = clip_masks(clip_lengths[0], rows)
    conv_rows = conv_weight.shape[0]
    mix_rows = mix_weight.shape[0]
    both = jnp.concatenate([conv_weight, mix_weight], axis=0)
    core = lax.axis_index("c")
    half = C // 2
    own = lax.all_gather(
        lax.dynamic_slice_in_dim(both, core * half, half, axis=1), "z", axis=0, tiled=True
    )
    audio_f = audio.astype(jnp.float32)
    act_in, slope_in, dalpha_in = snake_parts(audio_f, alpha_in)
    first = act_in.astype(jnp.bfloat16)
    columns = []
    for kernel_tap_index in range(TAPS):
        tap_offset = (kernel_tap_index - 3) * DILATION_SIZE
        moved = shift_rows(first, tap_offset, 0)
        columns.append(
            jnp.where(same_clip_flags[kernel_tap_index][:, None], moved, jnp.zeros_like(moved))
        )
    unfolded = jnp.concatenate(columns, axis=1)
    sizes = [lax.axis_size(a) for a in FRAME_AXES]
    devices = 1
    for s in sizes:
        devices *= s
    conv_each = unfolded.shape[1] // devices
    mix_each = C // devices
    order = [FRAME_AXES.index(a) for a in SCATTER_ORDER]

    def lay_out(left):
        left = jnp.concatenate(left, axis=2).reshape(rows, *sizes, conv_each + mix_each)
        return left.transpose(0, *[o + 1 for o in order], 5).reshape(rows, -1)

    conv_lhs = lay_out(
        [
            unfolded.reshape(rows, devices, conv_each),
            jnp.zeros((rows, devices, mix_each), unfolded.dtype),
        ]
    )
    own, conv_lhs = lax.optimization_barrier((own, conv_lhs))
    other = lax.ppermute(own, "c", [(0, 1), (1, 0)])
    first_half = jnp.where(core == 0, own, other)
    second_half = jnp.where(core == 0, other, own)
    gathered = jnp.concatenate([first_half, second_half], axis=1)
    gathered = gathered.reshape(-1, conv_rows + mix_rows, C)
    conv_full = gathered[:, :conv_rows].reshape(-1, C)
    mix_full = gathered[:, conv_rows:].reshape(-1, C)
    product = jnp.dot(unfolded, conv_full, preferred_element_type=jnp.float32)
    pre = product + conv_bias
    act_mid, slope_mid, dalpha_mid = snake_parts(pre, alpha_mid)
    second = act_mid.astype(jnp.bfloat16)
    second_gradient = lax.dot_general(
        cotangent, mix_full, (((1,), (1,)), ((), ())), preferred_element_type=jnp.float32
    )
    d_pre = (second_gradient * slope_mid).astype(jnp.bfloat16)
    d_unf = lax.dot_general(
        d_pre, conv_full, (((1,), (1,)), ((), ())), preferred_element_type=jnp.float32
    ).astype(jnp.bfloat16)
    d_first = jnp.zeros((rows, C), jnp.float32)
    for kernel_tap_index in range(TAPS):
        tap_offset = (kernel_tap_index - 3) * DILATION_SIZE
        piece = d_unf[:, kernel_tap_index * C : (kernel_tap_index + 1) * C].astype(jnp.float32)
        piece = jnp.where(same_clip_flags[kernel_tap_index][:, None], piece, jnp.zeros_like(piece))
        d_first = d_first + shift_rows(piece, -tap_offset, 0.0)
    in_grad = (cotangent.astype(jnp.float32) + d_first * slope_in).astype(jnp.bfloat16)
    vectors = jnp.stack(
        [
            jnp.sum(d_pre.astype(jnp.float32), axis=0),
            jnp.sum(cotangent.astype(jnp.float32), axis=0),
            jnp.sum(d_first * dalpha_in, axis=0),
            jnp.sum(second_gradient * dalpha_mid, axis=0),
        ]
    )
    mix_lhs = lay_out(
        [
            jnp.zeros((rows, devices, conv_each), second.dtype),
            second.reshape(rows, devices, mix_each),
        ]
    )
    packed = lax.dot_general(
        jnp.concatenate([conv_lhs, mix_lhs], axis=0),
        jnp.concatenate([d_pre, cotangent], axis=0),
        (((0,), (0,)), ((), ())),
        preferred_element_type=jnp.float32,
    )
    first_axis, second_axis, *rest = SCATTER_ORDER
    packed = lax.psum_scatter(
        packed.astype(jnp.bfloat16), first_axis, scatter_dimension=0, tiled=True
    )
    vectors = lax.psum(vectors, first_axis)
    packed, vectors = lax.optimization_barrier((packed, vectors))
    packed = lax.psum_scatter(packed, second_axis, scatter_dimension=0, tiled=True)
    packed = packed.astype(jnp.float32)
    vectors = lax.psum(vectors, second_axis)
    block = conv_each + mix_each
    held = packed.shape[0] // block
    share = vectors.shape[1] // devices
    vec_blocks = vectors.reshape(4, devices, share).transpose(1, 0, 2).reshape(*sizes, 4 * share)
    kept_names = list(FRAME_AXES)
    for axis in (first_axis, second_axis):
        position = kept_names.index(axis)
        vec_blocks = jnp.take(vec_blocks, lax.axis_index(axis), axis=position)
        kept_names.pop(position)
    vec_blocks = vec_blocks.transpose(*[kept_names.index(a) for a in rest], len(kept_names))
    vec_blocks = vec_blocks.reshape(held, 4 * share)
    extra = jnp.zeros((held, block, EXTRA_COLUMNS), jnp.float32)
    extra = extra.at[:, 0, : 4 * share].set(vec_blocks)
    packed = jnp.concatenate([packed.reshape(held, block, C), extra], axis=2)
    packed = packed.reshape(held * block, C + EXTRA_COLUMNS)
    for axis in rest:
        packed = permute_scatter(packed, axis)
    conv_grad = packed[:conv_each, :C]
    mix_grad = packed[conv_each:, :C]
    vector_grad = packed[0, C : C + 4 * share].reshape(4, share)
    return (in_grad, conv_grad, mix_grad, vector_grad)


def solution(mesh):
    devices = mesh.devices
    xs = len({d.coords[0] for d in devices.flat})
    ys = len({d.coords[1] for d in devices.flat})
    dp, shard = devices.shape
    split = Mesh(devices.reshape(xs, ys, dp // (xs * ys), shard), FRAME_AXES)
    frames = P(FRAME_AXES)
    placed = (frames, frames, frames, P("z", None), P("z", None), P(), P(), P())
    return jax.shard_map(
        per_device,
        mesh=split,
        in_specs=placed,
        out_specs=(frames, frames, frames, P(None, FRAME_AXES)),
        check_vma=False,
    )
```

profile of v0, /device:TPU:8, one launch (start us, length us, event | category | flops | bytes accessed | tf_op | source)
XLA Modules:
  0.0 164.8 jit_solution(2630460605486601233)
XLA Ops:
  7.2 1.7 %fusion.19 = bf16[512,256]{1,0:T(8,128)(2,1)} fusion(s32[]{:T(128)S(6)} %select_n.127, bf16[448,512]{1,0:T(8,128)(2,1)} %param.13, bf16[64,512]{1,0:T(8,128)(2,1)} %param.14), kind=kLoop, calls=%fused_computation.55 | loop fusion | flops 524288 | bytes 786436 | tf_op jit(solution)/shard_map/concatenate | solution.py:64
  9.0 0.8 reduce-window.8
  10.2 2.8 %fusion.10 = bf16[256,512]{1,0:T(8,128)(2,1)S(1)} fusion(bf16[256,512]{1,0:T(8,128)(2,1)} %param.10, f32[512]{0:T(512)} %param.16), kind=kLoop, calls=%fused_computation.31 | loop fusion | flops 786432 | bytes 526336 | tf_op jit(solution)/shard_map/convert_element_type | solution.py:72
  13.5 0.4 copy-done.1
  13.9 1.8 %constant_dynamic-update-slice_fusion = bf16[256,3584]{1,0:T(8,128)(2,1)S(1)} fusion(bf16[256,3584]{1,0:T(8,128)(2,1)S(1)} %select_dynamic-update-slice_fusion.3, f32[512]{0:T(512)S(1)} %copy-done.5, bf16[256,512]{1,0:T(8,128)(2,1)S(1)} %copy-done.1), kind=kLoop, calls=%fused_computation.72 | loop fusion | flops 786432 | bytes 526336
  16.1 1.3 copy-done.2
  17.4 2.3 %copy.34 = bf16[256,3584]{0,1:T(8,128)(2,1)} copy(bf16[256,3584]{1,0:T(8,128)(2,1)S(1)} %select_dynamic-update-slice_fusion) | data formatting | bytes 3670016 | tf_op jit(solution)/shard_map/concatenate | solution.py:80
  19.7 2.5 %reshape.128 = bf16[256,256,14]{0,2,1:T(8,128)(2,1)S(1)} reshape(bf16[256,3584]{0,1:T(8,128)(2,1)} %copy.34) | data formatting | bytes 3670016 | tf_op jit(solution)/shard_map/reshape | solution.py:95
  22.2 0.2 concatenate.97
  22.5 0.3 copy.35
  22.8 31.3 %all-gather.2.cloned.1.call-done = bf16[4096,256]{1,0:T(8,128)(2,1)} async-done(((bf16[512,256]{1,0:T(8,128)(2,1)}), bf16[4096,256]{1,0:T(8,128)(2,1)}) %all-gather.2.cloned.1.call-update) | async-done | bytes 2097168 | tf_op jit(solution)/shard_map/all_gather | solution.py:67
  54.1 4.5 %collective-permute-done = bf16[4096,256]{1,0:T(8,128)(2,1)} collective-permute-done((bf16[4096,256]{1,0:T(8,128)(2,1)}, bf16[4096,256]{1,0:T(8,128)(2,1)}, u32[]{:S(2)}, u32[]{:S(2)}) %collective-permute-start) | collective-permute-done | bytes 2097184 | tf_op jit(solution)/shard_map/ppermute | solution.py:100
  58.6 2.5 %broadcast_select_fusion.1 = (bf16[4096,256]{1,0:T(8,128)(2,1)S(1)}, bf16[4096,256]{1,0:T(8,128)(2,1)S(1)}) fusion(bf16[4096,256]{1,0:T(8,128)(2,1)} %all-gather.2.cloned.1.call-done, bf16[4096,256]{1,0:T(8,128)(2,1)} %collective-permute-done, pred[]{:T(512)S(6)} %eq.30), kind=kLoop, calls=%fused_computation.7 | loop fusion | flops 2097152 | bytes 8388609 | tf_op jit(solution)/shard_map/jit(_where)/select_n | solution.py:101
  61.1 0.3 pad_maximum_fusion
  61.5 0.2 slice.174
  61.8 1.8 %copy-done.3 = bf16[256,3584]{1,0:T(8,128)(2,1)S(1)} copy-done((bf16[256,3584]{1,0:T(8,128)(2,1)S(1)}, bf16[256,3584]{1,0:T(8,128)(2,1)}, u32[]{:S(2)}) %copy-start.3) | copy-done | bytes 1835032
  63.6 1.1 convolution_add_fusion
  64.7 4.1 %convert_reduce_fusion.1 = (f32[512]{0:T(512)S(1)}, bf16[256,512]{1,0:T(8,128)(2,1)S(1)}, f32[512]{0:T(512)S(1)}, bf16[256,512]{1,0:T(8,128)(2,1)S(1)}) fusion(f32[256,512]{1,0:T(8,128)S(1)} %convolution_add_fusion, f32[512]{0:T(512)S(1)} %get-tuple-element.90, f32[512]{0:T(512)S(1)} %get-tuple-element.91, f32[512]{0:T(512)S(1)} %copy-done.6, ...), kind=kOutput, calls=%fused_computation.42 | convolution fusion | flops 136444928 | bytes 1845248 | tf_op jit(solution)/shard_map/dot_general | solution.py:111
  69.1 0.5 concatenate.105
  69.5 0.3 copy.37
  69.8 4.4 %convolution_convert_fusion = bf16[4096,512]{1,0:T(8,128)(2,1)} fusion(bf16[256,4096]{0,1:T(8,128)(2,1)S(1)} %bitcast.52, bf16[256,4096]{0,1:T(8,128)(2,1)S(1)} %bitcast.51, bf16[256,512]{1,0:T(8,128)(2,1)S(1)} %copy-done.4, bf16[256,512]{1,0:T(8,128)(2,1)S(1)} %get-tuple-element.63), kind=kOutput, calls=%fused_computation | convolution fusion | flops 2159017984 | bytes 8912896 | tf_op jit(solution)/shard_map/dot_general | solution.py:139
  74.2 0.2 reduce-scatter.5.cloned.1.call-start
  74.7 3.2 %convolution_convert_fusion.1 = bf16[256,3584]{1,0:T(8,128)(2,1)S(1)} fusion(bf16[256,512]{1,0:T(8,128)(2,1)S(1)} %get-tuple-element.63, bf16[3584,512]{1,0:T(8,128)(2,1)} %bitcast.48), kind=kOutput, calls=%fused_computation.1 | convolution fusion | flops 940441600 | bytes 5767168 | tf_op jit(solution)/shard_map/dot_general | solution.py:115
  78.2 0.2 convert_select_fusion.2
  78.4 0.2 convert_select_fusion
  78.6 3.9 %fusion.18 = (f32[512]{0:T(512)S(1)}, f32[256,512]{1,0:T(8,128)S(1)}) fusion(bf16[256,512]{1,0:T(8,128)(2,1)S(1)} %copy-done.1, f32[512]{0:T(512)S(1)} %get-tuple-element.93, f32[512]{0:T(512)S(1)} %get-tuple-element.92, f32[512]{0:T(512)S(1)} %copy-done.5, f32[229,512]{1,0:T(8,128)S(1)} %get-tuple-element.110, f32[238,512]{1,0:T(8,128)S(1)} %get-tuple-element.108, ...), kind=kLoop, calls=%fused_computation.48 | loop fusion | flops 2227712 | bytes 3981312 | tf_op jit(solution)/shard_map/reduce_sum | solution.py:129
  82.5 2.5 %convert_reduce_fusion = (f32[512]{0:T(512)S(1)}, bf16[256,512]{1,0:T(8,128)(2,1)}) fusion(bf16[256,512]{1,0:T(8,128)(2,1)S(1)} %copy-done.4, f32[256,512]{1,0:T(8,128)S(1)} %get-tuple-element.65, bf16[256,512]{1,0:T(8,128)(2,1)S(1)} %copy-done.1, f32[512]{0:T(512)S(1)} %get-tuple-element.92), kind=kLoop, calls=%fused_computation.22 | loop fusion | flops 1048064 | bytes 1314816 | tf_op jit(solution)/shard_map/reduce_sum | solution.py:128
  85.0 2.5 %psum.14 = f32[4,512]{1,0:T(4,128)S(1)} all-reduce(f32[4,512]{1,0:T(4,128)S(1)} %pad_maximum_fusion.1), channel_id=1, replica_groups=mesh['x'=4,'y'=4,'c'=2,'z'=8] {'c'}, use_global_device_ids=true, to_apply=%region_7.8 | all-reduce | flops 2048 | bytes 16384 | tf_op jit(solution)/shard_map/psum | solution.py:149
  87.5 2.9 %reduce-scatter.3.cloned.1.call-done = bf16[2048,512]{1,0:T(8,128)(2,1)} async-done(((bf16[4096,512]{1,0:T(8,128)(2,1)}), bf16[2048,512]{1,0:T(8,128)(2,1)}) %reduce-scatter.3.cloned.1.call-update) | async-done | bytes 2097168 | tf_op jit(solution)/shard_map/reduce_scatter | solution.py:146
  90.8 0.3 reshape.138
  91.0 32.0 %psum.15 = f32[4,4,2,8,8]{3,2,1,0,4:T(2,128)S(1)} all-reduce(f32[4,4,2,8,8]{3,2,1,0,4:T(2,128)S(1)} %reshape.138), channel_id=1, replica_groups=mesh['x'=4,'y'=4,'c'=2,'z'=8] {'z'}, use_global_device_ids=true, to_apply=%region_9.10 | all-reduce | flops 2048 | bytes 16384 | tf_op jit(solution)/shard_map/psum | solution.py:153
  123.0 0.2 broadcast_select_fusion.3
  123.2 0.2 copy.44
  123.4 13.6 %reduce-scatter.5.cloned.1.call-done = bf16[256,512]{1,0:T(8,128)(2,1)} async-done(((bf16[2048,512]{1,0:T(8,128)(2,1)}), bf16[256,512]{1,0:T(8,128)(2,1)}) %reduce-scatter.5.cloned.1.call-update) | async-done | bytes 262160 | tf_op jit(solution)/shard_map/reduce_scatter | solution.py:151
  137.0 1.0 convert_element_type.72
  138.0 1.6 collective-permute-start.1
  139.6 1.5 collective-permute-start.2
  141.1 2.3 %collective-permute-start.3 = (f32[64,640]{1,0:T(8,128)S(1)}, f32[64,640]{1,0:T(8,128)S(1)}, u32[]{:S(2)}, u32[]{:S(2)}) collective-permute-start(f32[64,640]{1,0:T(8,128)S(1)} %get-tuple-element.77), channel_id=1, source_target_pairs={{0,48},{16,0},{32,16},{48,32},{1,49},{17,1},{33,17},{49,33},{2,50}... | collective-permute-start | bytes 491528 | tf_op jit(solution)/shard_map/ppermute | solution.py:53
  143.4 3.1 %collective-permute-done.2 = f32[64,640]{1,0:T(8,128)S(1)} collective-permute-done((f32[64,640]{1,0:T(8,128)S(1)}, f32[64,640]{1,0:T(8,128)S(1)}, u32[]{:S(2)}, u32[]{:S(2)}) %collective-permute-start.2) | collective-permute-done | bytes 163872 | tf_op jit(solution)/shard_map/ppermute | solution.py:53
  146.5 1.6 collective-permute-done.3
  148.2 1.2 collective-permute-start.4
  149.4 2.9 %collective-permute-start.5 = (f32[16,640]{1,0:T(8,128)S(1)}, f32[16,640]{1,0:T(8,128)S(1)}, u32[]{:S(2)}, u32[]{:S(2)}) collective-permute-start(f32[16,640]{1,0:T(8,128)S(1)} %get-tuple-element.89), channel_id=1, source_target_pairs={{0,128},{64,192},{128,0},{192,64},{1,129},{65,193},{129,1},{193,65... | collective-permute-start | bytes 122888 | tf_op jit(solution)/shard_map/ppermute | solution.py:53
  152.2 1.3 collective-permute-start.6
  153.5 1.3 collective-permute-done.5
  154.9 1.4 collective-permute-done.6
  156.3 0.6 slice.194
  156.9 0.6 slice.195
  157.6 0.7 copy.43
  (55 shorter events, 2.7 us)
Async XLA Ops:
  7.2 46.9 %all-gather.2.cloned.1.call-start = ((), (), s32[]{:S(2)}) async-start(), calls=%async_computation.2 | async-start | bytes 2359296 | tf_op jit(solution)/shard_map/all_gather | solution.py:67
  8.9 81.5 %reduce-scatter.3.cloned.1.call-start = ((), (), s32[]{:S(2)}) async-start(), calls=%async_computation.3 | async-start | bytes 6291456 | tf_op jit(solution)/shard_map/reduce_scatter | solution.py:146
  12.9 1.0 copy-start.1
  12.9 0.9 copy-start.5
  16.1 1.3 copy-start.2
  22.5 31.7 %copy-start.6 = (f32[512]{0:T(512)S(1)}, f32[512]{0:T(512)}, u32[]{:S(2)}) copy-start(f32[512]{0:T(512)} %param.17) | copy-start | bytes 6148
  54.1 4.5 %collective-permute-start = (bf16[4096,256]{1,0:T(8,128)(2,1)}, bf16[4096,256]{1,0:T(8,128)(2,1)}, u32[]{:S(2)}, u32[]{:S(2)}) collective-permute-start(bf16[4096,256]{1,0:T(8,128)(2,1)} %all-gather.2.cloned.1.call-done), channel_id=1, source_target_pairs={{0,8},{8,0},{1,9},{9,1},{2,10},{10,2},{3,11},{11,3},{4,12},{12,4},... | collective-permute-start | bytes 6291464 | tf_op jit(solution)/shard_map/ppermute | solution.py:100
  61.4 2.2 %copy-start.3 = (bf16[256,3584]{1,0:T(8,128)(2,1)S(1)}, bf16[256,3584]{1,0:T(8,128)(2,1)}, u32[]{:S(2)}) copy-start(bf16[256,3584]{1,0:T(8,128)(2,1)} %copy-done.2) | copy-start | bytes 5505028
  61.5 2.2 %copy-start.7 = (f32[512]{0:T(512)S(1)}, f32[512]{0:T(512)}, u32[]{:S(2)}) copy-start(f32[512]{0:T(512)} %param.15) | copy-start | bytes 6148
  61.7 3.0 %copy-start = (bf16[8,448,512]{2,1,0:T(8,128)(2,1)}, bf16[8,448,512]{2,1,0:T(8,128)(2,1)S(1)}, u32[]{:S(2)}) copy-start(bf16[8,448,512]{2,1,0:T(8,128)(2,1)S(1)} %slice.174) | copy-start | bytes 11010052
  63.6 1.1 copy-start.4
  74.2 62.7 %reduce-scatter.5.cloned.1.call-start = ((), (), s32[]{:S(2)}) async-start(), calls=%async_computation.4 | async-start | bytes 2359296 | tf_op jit(solution)/shard_map/reduce_scatter | solution.py:151
  138.0 5.4 %collective-permute-start.1 = (f32[64,640]{1,0:T(8,128)S(1)}, f32[64,640]{1,0:T(8,128)S(1)}, u32[]{:S(2)}, u32[]{:S(2)}) collective-permute-start(f32[64,640]{1,0:T(8,128)S(1)} %get-tuple-element.75), channel_id=1, source_target_pairs={{0,16},{16,32},{32,48},{48,0},{1,17},{17,33},{33,49},{49,1},{2,18}... | collective-permute-start | bytes 491528 | tf_op jit(solution)/shard_map/ppermute | solution.py:53
  139.6 6.9 %collective-permute-start.2 = (f32[64,640]{1,0:T(8,128)S(1)}, f32[64,640]{1,0:T(8,128)S(1)}, u32[]{:S(2)}, u32[]{:S(2)}) collective-permute-start(f32[64,640]{1,0:T(8,128)S(1)} %get-tuple-element.76), channel_id=1, source_target_pairs={{0,32},{16,48},{32,0},{48,16},{1,33},{17,49},{33,1},{49,17},{2,34}... | collective-permute-start | bytes 491528 | tf_op jit(solution)/shard_map/ppermute | solution.py:53
  141.1 7.1 %collective-permute-start.3 = (f32[64,640]{1,0:T(8,128)S(1)}, f32[64,640]{1,0:T(8,128)S(1)}, u32[]{:S(2)}, u32[]{:S(2)}) collective-permute-start(f32[64,640]{1,0:T(8,128)S(1)} %get-tuple-element.77), channel_id=1, source_target_pairs={{0,48},{16,0},{32,16},{48,32},{1,49},{17,1},{33,17},{49,33},{2,50}... | collective-permute-start | bytes 491528 | tf_op jit(solution)/shard_map/ppermute | solution.py:53
  148.2 5.3 %collective-permute-start.4 = (f32[16,640]{1,0:T(8,128)S(1)}, f32[16,640]{1,0:T(8,128)S(1)}, u32[]{:S(2)}, u32[]{:S(2)}) collective-permute-start(f32[16,640]{1,0:T(8,128)S(1)} %get-tuple-element.87), channel_id=1, source_target_pairs={{0,64},{64,128},{128,192},{192,0},{1,65},{65,129},{129,193},{193,1... | collective-permute-start | bytes 122888 | tf_op jit(solution)/shard_map/ppermute | solution.py:53
  149.4 5.5 %collective-permute-start.5 = (f32[16,640]{1,0:T(8,128)S(1)}, f32[16,640]{1,0:T(8,128)S(1)}, u32[]{:S(2)}, u32[]{:S(2)}) collective-permute-start(f32[16,640]{1,0:T(8,128)S(1)} %get-tuple-element.89), channel_id=1, source_target_pairs={{0,128},{64,192},{128,0},{192,64},{1,129},{65,193},{129,1},{193,65... | collective-permute-start | bytes 122888 | tf_op jit(solution)/shard_map/ppermute | solution.py:53
  152.2 4.0 %collective-permute-start.6 = (f32[16,640]{1,0:T(8,128)S(1)}, f32[16,640]{1,0:T(8,128)S(1)}, u32[]{:S(2)}, u32[]{:S(2)}) collective-permute-start(f32[16,640]{1,0:T(8,128)S(1)} %get-tuple-element.88), channel_id=1, source_target_pairs={{0,192},{64,0},{128,64},{192,128},{1,193},{65,1},{129,65},{193,129... | collective-permute-start | bytes 122888 | tf_op jit(solution)/shard_map/ppermute | solution.py:53
Sparse Core Ops, SparseCore 0:
  10.3 43.7 all-gather.1
  74.4 16.0 reduce-scatter.2
  93.0 43.9 reduce-scatter.4
where the time goes:
time: 165 us
  waiting for transfers between devices  59.8 us (36%)
  blocking collectives  34.5 us (21%)
  other arithmetic  19 us (12%)
  between operations  14.2 us (9%)
  local copies, waits for them, and re-layouts  13.6 us (8%)
  matrix products  12.7 us (8%)
  starting transfers between devices  11 us (7%)
    psum x1, blocking collectives, per_device(): vectors = lax.psum(vectors, second_axis)  32 us
    all_gather x1, waiting for transfers between devices, per_device(): lax.all_gather(lax.dynamic_slice_in_dim(both, core * half, half, axis=1),...  31.3 us
    reduce_scatter x1, waiting for transfers between devices, per_device(): lax.psum_scatter(packed, second_axis, scatter_dimension=0, tiled=True)  13.6 us
    ppermute x6, starting transfers between devices, permute_scatter(): lax.ppermute(chunk, axis, [(j, (j + step) % n) for j in range(n)])  10.7 us
    ppermute x6, waiting for transfers between devices, permute_scatter(): lax.ppermute(chunk, axis, [(j, (j + step) % n) for j in range(n)])  7.47 us
    ppermute x1, waiting for transfers between devices, per_device(): other = lax.ppermute(own, 'c', [(0, 1), (1, 0)])  4.49 us
    dot_general x1, matrix products, per_device(): lax.dot_general(jnp.concatenate([conv_lhs, mix_lhs], axis=0), jnp.concate...  4.38 us
    unnamed x17, local copies, waits for them, and re-layouts  4.23 us
  transfers between devices with their start and end apart: 10, of which 8 were waited for; matrix products, arithmetic and copies ran while one was open for 14% of the time, Pallas kernels for 0%

commit v1 on v0

--- a/solution.py
+++ b/solution.py
@@ -64,8 +64,16 @@
     both = jnp.concatenate([conv_weight, mix_weight], axis=0)
     core = lax.axis_index("c")
     half = C // 2
-    own = lax.all_gather(
-        lax.dynamic_slice_in_dim(both, core * half, half, axis=1), "z", axis=0, tiled=True
+    own = jnp.concatenate(
+        lax.all_to_all(
+            jnp.stack(
+                [lax.dynamic_slice_in_dim(both, core * half, half, axis=1)] * lax.axis_size("z")
+            ),
+            "z",
+            0,
+            0,
+        ),
+        axis=0,
     )
     audio_f = audio.astype(jnp.float32)
     act_in, slope_in, dalpha_in = snake_parts(audio_f, alpha_in)

time: 165 us -> 179 us (1.085)
  starting transfers between devices: 11 us -> 19.2 us
  waiting for transfers between devices: 59.8 us -> 66.2 us
  other arithmetic: 19 us -> 16.7 us
    all_to_all x0 -> x1, waiting for transfers between devices: none -> 39.4 us  [per_device(): lax.all_to_all(jnp.stack([lax.dynamic_slice_in_dim(both, core * half, hal...]
    all_gather x1 -> x0, waiting for transfers between devices: 31.3 us -> none  [per_device(): lax.all_gather(lax.dynamic_slice_in_dim(both, core * half, half, axis=1),...]
    all_to_all x0 -> x1, starting transfers between devices: none -> 8.6 us  [per_device(): lax.all_to_all(jnp.stack([lax.dynamic_slice_in_dim(both, core * half, hal...]
    reduce_scatter x1, waiting for transfers between devices: 2.9 us -> 0.61 us  [per_device(): lax.psum_scatter(packed.astype(jnp.bfloat16), first_axis, scatter_dimensi...]
    unnamed x17 -> x19, local copies, waits for them, and re-layouts: 4.23 us -> 3.86 us
  transfers between devices with their start and end apart: 10 -> 10, of which waited for: 8 -> 9; matrix products, arithmetic and copies ran while one was open for 14% -> 12% of each run, Pallas kernels for 0% -> 0%
where the time goes in v1:
time: 179 us
  waiting for transfers between devices  66.2 us (37%)
  blocking collectives  34.4 us (19%)
  starting transfers between devices  19.2 us (11%)
  other arithmetic  16.7 us (9%)
  local copies, waits for them, and re-layouts  14.7 us (8%)
  between operations  14.5 us (8%)
  matrix products  12.8 us (7%)
    all_to_all x1, waiting for transfers between devices, per_device(): lax.all_to_all(jnp.stack([lax.dynamic_slice_in_dim(both, core * half, hal...  39.4 us
    psum x1, blocking collectives, per_device(): vectors = lax.psum(vectors, second_axis)  31.9 us
    reduce_scatter x1, waiting for transfers between devices, per_device(): lax.psum_scatter(packed, second_axis, scatter_dimension=0, tiled=True)  13.6 us
    ppermute x6, starting transfers between devices, permute_scatter(): lax.ppermute(chunk, axis, [(j, (j + step) % n) for j in range(n)])  10.3 us
    all_to_all x1, starting transfers between devices, per_device(): lax.all_to_all(jnp.stack([lax.dynamic_slice_in_dim(both, core * half, hal...  8.6 us
    ppermute x6, waiting for transfers between devices, permute_scatter(): lax.ppermute(chunk, axis, [(j, (j + step) % n) for j in range(n)])  8.12 us
    ppermute x1, waiting for transfers between devices, per_device(): other = lax.ppermute(own, 'c', [(0, 1), (1, 0)])  4.48 us
    dot_general x1, matrix products, per_device(): lax.dot_general(jnp.concatenate([conv_lhs, mix_lhs], axis=0), jnp.concate...  4.39 us
  transfers between devices with their start and end apart: 10, of which 9 were waited for; matrix products, arithmetic and copies ran while one was open for 12% of the time, Pallas kernels for 0%

profile of v1, /device:TPU:8, one launch (start us, length us, event | category | flops | bytes accessed | tf_op | source)
XLA Modules:
  0.0 178.5 jit_solution(8204874767437501839)
XLA Ops:
  7.2 1.0 fusion.19
  8.1 1.5 stack.12
  9.6 8.6 %all-to-all-start = ((bf16[8,512,256]{2,1,0:T(8,128)(2,1)}), bf16[8,512,256]{2,1,0:T(8,128)(2,1)}, u32[]{:S(2)}, u32[]{:S(2)}) async-start(bf16[8,512,256]{2,1,0:T(8,128)(2,1)} %stack.12), calls=%async_computation | async-start | bytes 4194304 | tf_op jit(solution)/shard_map/all_to_all | solution.py:68
  18.3 0.2 reduce-window.8
  18.8 1.8 %fusion.10 = bf16[256,512]{1,0:T(8,128)(2,1)S(1)} fusion(bf16[256,512]{1,0:T(8,128)(2,1)S(1)} %copy-done.1, f32[512]{0:T(512)S(1)} %copy-done.5), kind=kLoop, calls=%fused_computation.31 | loop fusion | flops 786432 | bytes 526336 | tf_op jit(solution)/shard_map/convert_element_type | solution.py:80
  21.2 1.8 %constant_dynamic-update-slice_fusion = bf16[256,3584]{1,0:T(8,128)(2,1)S(1)} fusion(bf16[256,3584]{1,0:T(8,128)(2,1)S(1)} %select_dynamic-update-slice_fusion.3, f32[512]{0:T(512)S(1)} %copy-done.5, bf16[256,512]{1,0:T(8,128)(2,1)S(1)} %copy-done.1), kind=kLoop, calls=%fused_computation.72 | loop fusion | flops 786432 | bytes 526336
  23.5 1.3 copy-done.2
  24.8 2.3 %copy.34 = bf16[256,3584]{0,1:T(8,128)(2,1)} copy(bf16[256,3584]{1,0:T(8,128)(2,1)S(1)} %select_dynamic-update-slice_fusion) | data formatting | bytes 3670016 | tf_op jit(solution)/shard_map/concatenate | solution.py:88
  27.1 2.5 %reshape.134 = bf16[256,256,14]{0,2,1:T(8,128)(2,1)S(1)} reshape(bf16[256,3584]{0,1:T(8,128)(2,1)} %copy.34) | data formatting | bytes 3670016 | tf_op jit(solution)/shard_map/reshape | solution.py:103
  29.6 0.2 concatenate.97
  29.8 0.3 copy.35
  30.1 39.4 %all-to-all-done = bf16[8,512,256]{2,1,0:T(8,128)(2,1)} async-done(((bf16[8,512,256]{2,1,0:T(8,128)(2,1)}), bf16[8,512,256]{2,1,0:T(8,128)(2,1)}, u32[]{:S(2)}, u32[]{:S(2)}) %all-to-all-start) | async-done | bytes 2097184 | tf_op jit(solution)/shard_map/all_to_all | solution.py:68
  69.5 4.5 %collective-permute-done = bf16[4096,256]{1,0:T(8,128)(2,1)} collective-permute-done((bf16[4096,256]{1,0:T(8,128)(2,1)}, bf16[4096,256]{1,0:T(8,128)(2,1)}, u32[]{:S(2)}, u32[]{:S(2)}) %collective-permute-start) | collective-permute-done | bytes 2097184 | tf_op jit(solution)/shard_map/ppermute | solution.py:108
  74.0 2.5 %broadcast_select_fusion.1 = (bf16[4096,256]{1,0:T(8,128)(2,1)S(1)}, bf16[4096,256]{1,0:T(8,128)(2,1)S(1)}) fusion(bf16[4096,256]{1,0:T(8,128)(2,1)} %bitcast.2, bf16[4096,256]{1,0:T(8,128)(2,1)} %collective-permute-done, pred[]{:T(512)S(6)} %eq.30), kind=kLoop, calls=%fused_computation.7 | loop fusion | flops 2097152 | bytes 8388609 | tf_op jit(solution)/shard_map/jit(_where)/select_n | solution.py:109
  76.5 0.3 pad_maximum_fusion
  76.9 0.2 slice.174
  77.2 1.8 %copy-done.3 = bf16[256,3584]{1,0:T(8,128)(2,1)S(1)} copy-done((bf16[256,3584]{1,0:T(8,128)(2,1)S(1)}, bf16[256,3584]{1,0:T(8,128)(2,1)}, u32[]{:S(2)}) %copy-start.3) | copy-done | bytes 1835032
  79.0 1.1 convolution_add_fusion
  80.1 4.1 %convert_reduce_fusion.1 = (f32[512]{0:T(512)S(1)}, bf16[256,512]{1,0:T(8,128)(2,1)S(1)}, f32[512]{0:T(512)S(1)}, bf16[256,512]{1,0:T(8,128)(2,1)S(1)}) fusion(f32[256,512]{1,0:T(8,128)S(1)} %convolution_add_fusion, f32[512]{0:T(512)S(1)} %get-tuple-element.90, f32[512]{0:T(512)S(1)} %get-tuple-element.91, f32[512]{0:T(512)S(1)} %copy-done.6, ...), kind=kOutput, calls=%fused_computation.42 | convolution fusion | flops 136444928 | bytes 1845248 | tf_op jit(solution)/shard_map/dot_general | solution.py:119
  84.5 0.5 concatenate.105
  84.9 0.3 copy.37
  85.2 4.4 %convolution_convert_fusion = bf16[4096,512]{1,0:T(8,128)(2,1)} fusion(bf16[256,4096]{0,1:T(8,128)(2,1)S(1)} %bitcast.53, bf16[256,4096]{0,1:T(8,128)(2,1)S(1)} %bitcast.52, bf16[256,512]{1,0:T(8,128)(2,1)S(1)} %copy-done.4, bf16[256,512]{1,0:T(8,128)(2,1)S(1)} %get-tuple-element.63), kind=kOutput, calls=%fused_computation | convolution fusion | flops 2159017984 | bytes 8912896 | tf_op jit(solution)/shard_map/dot_general | solution.py:147
  89.7 0.2 reduce-scatter.5.cloned.1.call-start
  90.1 3.2 %convolution_convert_fusion.1 = bf16[256,3584]{1,0:T(8,128)(2,1)S(1)} fusion(bf16[256,512]{1,0:T(8,128)(2,1)S(1)} %get-tuple-element.63, bf16[3584,512]{1,0:T(8,128)(2,1)} %bitcast.49), kind=kOutput, calls=%fused_computation.1 | convolution fusion | flops 940441600 | bytes 5767168 | tf_op jit(solution)/shard_map/dot_general | solution.py:123
  93.8 0.2 convert_select_fusion
  94.0 3.9 %fusion.18 = (f32[512]{0:T(512)S(1)}, f32[256,512]{1,0:T(8,128)S(1)}) fusion(bf16[256,512]{1,0:T(8,128)(2,1)S(1)} %copy-done.1, f32[512]{0:T(512)S(1)} %get-tuple-element.93, f32[512]{0:T(512)S(1)} %get-tuple-element.92, f32[512]{0:T(512)S(1)} %copy-done.5, f32[229,512]{1,0:T(8,128)S(1)} %get-tuple-element.110, f32[238,512]{1,0:T(8,128)S(1)} %get-tuple-element.108, ...), kind=kLoop, calls=%fused_computation.48 | loop fusion | flops 2227712 | bytes 3981312 | tf_op jit(solution)/shard_map/reduce_sum | solution.py:137
  97.9 2.5 %convert_reduce_fusion = (f32[512]{0:T(512)S(1)}, bf16[256,512]{1,0:T(8,128)(2,1)}) fusion(bf16[256,512]{1,0:T(8,128)(2,1)S(1)} %copy-done.4, f32[256,512]{1,0:T(8,128)S(1)} %get-tuple-element.65, bf16[256,512]{1,0:T(8,128)(2,1)S(1)} %copy-done.1, f32[512]{0:T(512)S(1)} %get-tuple-element.92), kind=kLoop, calls=%fused_computation.22 | loop fusion | flops 1048064 | bytes 1314816 | tf_op jit(solution)/shard_map/reduce_sum | solution.py:136
  100.4 2.5 %psum.14 = f32[4,512]{1,0:T(4,128)S(1)} all-reduce(f32[4,512]{1,0:T(4,128)S(1)} %pad_maximum_fusion.1), channel_id=1, replica_groups=mesh['x'=4,'y'=4,'c'=2,'z'=8] {'c'}, use_global_device_ids=true, to_apply=%region_7.8 | all-reduce | flops 2048 | bytes 16384 | tf_op jit(solution)/shard_map/psum | solution.py:157
  102.9 0.6 reduce-scatter.3.cloned.1.call-done
  103.9 0.3 reshape.144
  104.2 31.9 %psum.15 = f32[4,4,2,8,8]{3,2,1,0,4:T(2,128)S(1)} all-reduce(f32[4,4,2,8,8]{3,2,1,0,4:T(2,128)S(1)} %reshape.144), channel_id=1, replica_groups=mesh['x'=4,'y'=4,'c'=2,'z'=8] {'z'}, use_global_device_ids=true, to_apply=%region_9.10 | all-reduce | flops 2048 | bytes 16384 | tf_op jit(solution)/shard_map/psum | solution.py:161
  136.1 0.2 broadcast_select_fusion.3
  136.5 13.6 %reduce-scatter.5.cloned.1.call-done = bf16[256,512]{1,0:T(8,128)(2,1)} async-done(((bf16[2048,512]{1,0:T(8,128)(2,1)}), bf16[256,512]{1,0:T(8,128)(2,1)}) %reduce-scatter.5.cloned.1.call-update) | async-done | bytes 262160 | tf_op jit(solution)/shard_map/reduce_scatter | solution.py:159
  150.1 1.0 convert_element_type.72
  151.2 1.6 collective-permute-start.1
  152.8 1.2 collective-permute-start.2
  153.9 2.0 %collective-permute-start.3 = (f32[64,640]{1,0:T(8,128)S(1)}, f32[64,640]{1,0:T(8,128)S(1)}, u32[]{:S(2)}, u32[]{:S(2)}) collective-permute-start(f32[64,640]{1,0:T(8,128)S(1)} %get-tuple-element.77), channel_id=1, source_target_pairs={{0,48},{16,0},{32,16},{48,32},{1,49},{17,1},{33,17},{49,33},{2,50}... | collective-permute-start | bytes 491528 | tf_op jit(solution)/shard_map/ppermute | solution.py:53
  155.9 0.7 collective-permute-done.1
  156.6 3.1 %collective-permute-done.2 = f32[64,640]{1,0:T(8,128)S(1)} collective-permute-done((f32[64,640]{1,0:T(8,128)S(1)}, f32[64,640]{1,0:T(8,128)S(1)}, u32[]{:S(2)}, u32[]{:S(2)}) %collective-permute-start.2) | collective-permute-done | bytes 163872 | tf_op jit(solution)/shard_map/ppermute | solution.py:53
  159.7 1.3 collective-permute-done.3
  161.1 1.4 collective-permute-start.4
  162.5 3.2 %collective-permute-start.5 = (f32[16,640]{1,0:T(8,128)S(1)}, f32[16,640]{1,0:T(8,128)S(1)}, u32[]{:S(2)}, u32[]{:S(2)}) collective-permute-start(f32[16,640]{1,0:T(8,128)S(1)} %get-tuple-element.89), channel_id=1, source_target_pairs={{0,128},{64,192},{128,0},{192,64},{1,129},{65,193},{129,1},{193,65... | collective-permute-start | bytes 122888 | tf_op jit(solution)/shard_map/ppermute | solution.py:53
  165.7 1.0 collective-permute-start.6
  166.7 1.4 collective-permute-done.5
  168.1 1.6 collective-permute-done.6
  169.7 0.6 slice.194
  170.3 0.6 slice.195
  171.0 0.7 copy.43
  (57 shorter events, 3.0 us)
Async XLA Ops:
  9.6 8.6 %copy-start.8 = (s32[1,8]{1,0:T(1,128)S(1)}, s32[1,8]{1,0:T(1,128)}, u32[]{:S(2)}) copy-start(s32[1,8]{1,0:T(1,128)} %param.12) | copy-start | bytes 100
  9.6 9.2 %copy-start.1 = (bf16[256,512]{1,0:T(8,128)(2,1)S(1)}, bf16[256,512]{1,0:T(8,128)(2,1)}, u32[]{:S(2)}) copy-start(bf16[256,512]{1,0:T(8,128)(2,1)} %param.10) | copy-start | bytes 786436
  9.6 9.2 %copy-start.5 = (f32[512]{0:T(512)S(1)}, f32[512]{0:T(512)}, u32[]{:S(2)}) copy-start(f32[512]{0:T(512)} %param.16) | copy-start | bytes 6148
  9.6 59.9 %all-to-all-start = ((bf16[8,512,256]{2,1,0:T(8,128)(2,1)}), bf16[8,512,256]{2,1,0:T(8,128)(2,1)}, u32[]{:S(2)}, u32[]{:S(2)}) async-start(bf16[8,512,256]{2,1,0:T(8,128)(2,1)} %stack.12), calls=%async_computation | async-start | bytes 4194304 | tf_op jit(solution)/shard_map/all_to_all | solution.py:68
  18.2 85.3 %reduce-scatter.3.cloned.1.call-start = ((), (), s32[]{:S(2)}) async-start(), calls=%async_computation.3 | async-start | bytes 6291456 | tf_op jit(solution)/shard_map/reduce_scatter | solution.py:154
  23.5 1.3 copy-start.2
  29.8 39.7 %copy-start.6 = (f32[512]{0:T(512)S(1)}, f32[512]{0:T(512)}, u32[]{:S(2)}) copy-start(f32[512]{0:T(512)} %param.17) | copy-start | bytes 6148
  69.5 4.5 %collective-permute-start = (bf16[4096,256]{1,0:T(8,128)(2,1)}, bf16[4096,256]{1,0:T(8,128)(2,1)}, u32[]{:S(2)}, u32[]{:S(2)}) collective-permute-start(bf16[4096,256]{1,0:T(8,128)(2,1)} %bitcast.2), channel_id=1, source_target_pairs={{0,8},{8,0},{1,9},{9,1},{2,10},{10,2},{3,11},{11,3},{4,12},{12,4},... | collective-permute-start | bytes 6291464 | tf_op jit(solution)/shard_map/ppermute | solution.py:108
  76.8 2.2 %copy-start.3 = (bf16[256,3584]{1,0:T(8,128)(2,1)S(1)}, bf16[256,3584]{1,0:T(8,128)(2,1)}, u32[]{:S(2)}) copy-start(bf16[256,3584]{1,0:T(8,128)(2,1)} %copy-done.2) | copy-start | bytes 5505028
  76.9 2.2 %copy-start.7 = (f32[512]{0:T(512)S(1)}, f32[512]{0:T(512)}, u32[]{:S(2)}) copy-start(f32[512]{0:T(512)} %param.15) | copy-start | bytes 6148
  77.1 3.0 %copy-start = (bf16[8,448,512]{2,1,0:T(8,128)(2,1)}, bf16[8,448,512]{2,1,0:T(8,128)(2,1)S(1)}, u32[]{:S(2)}) copy-start(bf16[8,448,512]{2,1,0:T(8,128)(2,1)S(1)} %slice.174) | copy-start | bytes 11010052
  79.0 1.1 copy-start.4
  89.7 60.4 %reduce-scatter.5.cloned.1.call-start = ((), (), s32[]{:S(2)}) async-start(), calls=%async_computation.4 | async-start | bytes 2359296 | tf_op jit(solution)/shard_map/reduce_scatter | solution.py:159
  151.2 5.4 %collective-permute-start.1 = (f32[64,640]{1,0:T(8,128)S(1)}, f32[64,640]{1,0:T(8,128)S(1)}, u32[]{:S(2)}, u32[]{:S(2)}) collective-permute-start(f32[64,640]{1,0:T(8,128)S(1)} %get-tuple-element.75), channel_id=1, source_target_pairs={{0,16},{16,32},{32,48},{48,0},{1,17},{17,33},{33,49},{49,1},{2,18}... | collective-permute-start | bytes 491528 | tf_op jit(solution)/shard_map/ppermute | solution.py:53
  152.8 6.9 %collective-permute-start.2 = (f32[64,640]{1,0:T(8,128)S(1)}, f32[64,640]{1,0:T(8,128)S(1)}, u32[]{:S(2)}, u32[]{:S(2)}) collective-permute-start(f32[64,640]{1,0:T(8,128)S(1)} %get-tuple-element.76), channel_id=1, source_target_pairs={{0,32},{16,48},{32,0},{48,16},{1,33},{17,49},{33,1},{49,17},{2,34}... | collective-permute-start | bytes 491528 | tf_op jit(solution)/shard_map/ppermute | solution.py:53
  153.9 7.1 %collective-permute-start.3 = (f32[64,640]{1,0:T(8,128)S(1)}, f32[64,640]{1,0:T(8,128)S(1)}, u32[]{:S(2)}, u32[]{:S(2)}) collective-permute-start(f32[64,640]{1,0:T(8,128)S(1)} %get-tuple-element.77), channel_id=1, source_target_pairs={{0,48},{16,0},{32,16},{48,32},{1,49},{17,1},{33,17},{49,33},{2,50}... | collective-permute-start | bytes 491528 | tf_op jit(solution)/shard_map/ppermute | solution.py:53
  161.1 5.6 %collective-permute-start.4 = (f32[16,640]{1,0:T(8,128)S(1)}, f32[16,640]{1,0:T(8,128)S(1)}, u32[]{:S(2)}, u32[]{:S(2)}) collective-permute-start(f32[16,640]{1,0:T(8,128)S(1)} %get-tuple-element.87), channel_id=1, source_target_pairs={{0,64},{64,128},{128,192},{192,0},{1,65},{65,129},{129,193},{193,1... | collective-permute-start | bytes 122888 | tf_op jit(solution)/shard_map/ppermute | solution.py:53
  162.5 5.7 %collective-permute-start.5 = (f32[16,640]{1,0:T(8,128)S(1)}, f32[16,640]{1,0:T(8,128)S(1)}, u32[]{:S(2)}, u32[]{:S(2)}) collective-permute-start(f32[16,640]{1,0:T(8,128)S(1)} %get-tuple-element.89), channel_id=1, source_target_pairs={{0,128},{64,192},{128,0},{192,64},{1,129},{65,193},{129,1},{193,65... | collective-permute-start | bytes 122888 | tf_op jit(solution)/shard_map/ppermute | solution.py:53
  165.7 4.0 %collective-permute-start.6 = (f32[16,640]{1,0:T(8,128)S(1)}, f32[16,640]{1,0:T(8,128)S(1)}, u32[]{:S(2)}, u32[]{:S(2)}) collective-permute-start(f32[16,640]{1,0:T(8,128)S(1)} %get-tuple-element.88), channel_id=1, source_target_pairs={{0,192},{64,0},{128,64},{192,128},{1,193},{65,1},{129,65},{193,129... | collective-permute-start | bytes 122888 | tf_op jit(solution)/shard_map/ppermute | solution.py:53
Sparse Core Ops, SparseCore 0:
  89.8 13.7 reduce-scatter.2
  106.1 43.9 reduce-scatter.4
